TPU v7x, 256 devices: a whole 4x4x8 slice. The times are simulated.
256 devices in a mesh: dp: 32 (over y, x, core), tensor: 8 (over z).
Axes of the slice: x: 4, y: 4, z: 8, core: 2. Of those that a mesh axis runs over, the one named last changes fastest.
Arguments:
- tokens: bfloat16 [8192, 8192], P('dp'), may hold values from -6 to 6
- router_weight: bfloat16 [8192, 32], replicated, may hold values from -0.0625 to 0.0625
- gate_weight: bfloat16 [14336, 8192], P(('dp', 'tensor')), may hold values from -0.0625 to 0.0625
- up_weight: bfloat16 [14336, 8192], P(('dp', 'tensor')), may hold values from -0.0625 to 0.0625
- down_weight: bfloat16 [14336, 8192], P(('dp', 'tensor')), may hold values from -0.25 to 0.25
- cluster_of: int32 [14336, 1], P('dp'), may hold values from 0 to 31; in each aligned block of 448 rows (0 to 447, 448 to 895, ...) at most 28 rows name the same one
- expert_ids: int32 [8192, 2], P('dp'), may hold values from 0 to 31, all different within a row; in each aligned block of 256 rows (0 to 255, 256 to 511, ...) at most 32 rows name the same one
Outputs:
- mixed_out: bfloat16 [8192, 8192], P('dp', 'tensor')
Inputs may be any that keep to these rules, and one draw needn't show every extreme that they name: `expert_ids`: in each aligned block of 256 rows (the tokens of one dp index) no expert is named by more than 32 rows, a bound that some block reaches; a row names two different experts; every expert is named somewhere. `cluster_of`: in each aligned block of 448 hidden units no cluster holds more than 28 units, and some cluster holds exactly 28; every cluster holds some unit.
All inputs are finite; a program needn't handle non-finite values.
Results may differ from a plain program's by a relative error of at most 0.023.
Values may be sent and summed in bfloat16 or wider, within the bound.
No kernel may reach another device: no remote copies, remote signals or barrier semaphores. Data moves between devices by JAX's collectives and lax.ppermute only.
A program may use at most 64 MiB of HBM per device.

v0:
```python
import jax
import jax.numpy as jnp
from jax import lax
from jax.sharding import PartitionSpec as P


def place_rows(labels, bin_count, capacity):
    count_rows = labels.shape[0]
    onehot = (labels[:, None] == jnp.arange(bin_count, dtype=jnp.int32)[None, :]).astype(jnp.int32)
    before = jnp.cumsum(onehot, axis=0) - onehot
    rank_in = jnp.sum(before * onehot, axis=1)
    position = labels * capacity + rank_in
    slot_list = jnp.full((bin_count * capacity,), count_rows, jnp.int32)
    slot_list = slot_list.at[position].set(jnp.arange(count_rows, dtype=jnp.int32))
    return (slot_list, position)


def with_zero_row(matrix):
    pad = jnp.zeros((1,) + matrix.shape[1:], matrix.dtype)
    return jnp.concatenate([matrix, pad], axis=0)


def against(left_side, right_side):
    return lax.dot_general(
        left_side, right_side, (((1,), (1,)), ((), ())), preferred_element_type=jnp.float32
    )


def on_device(tokens, router_weight, gate_weight, up_weight, down_weight, cluster_of, expert_ids):
    owners = lax.axis_size("dp")
    tensor_count = lax.axis_size("tensor")
    width_part = tokens.shape[1] // tensor_count
    token_count = tokens.shape[0]
    logits = jnp.dot(tokens, router_weight, preferred_element_type=jnp.float32)
    scores = jax.nn.sigmoid(jnp.take_along_axis(logits, expert_ids, axis=1))
    mixing = scores / jnp.sum(scores, axis=1, keepdims=True)
    stacked = jnp.stack([gate_weight, up_weight, down_weight], axis=1)
    rows = lax.all_to_all(stacked, "tensor", split_axis=2, concat_axis=0, tiled=True)
    unit_cap = 2 * rows.shape[0] // owners
    unit_list, unit_spot = place_rows(cluster_of[:, 0], owners, unit_cap)
    pick = with_zero_row(rows)[unit_list]
    own = lax.all_to_all(pick, "dp", split_axis=0, concat_axis=0, tiled=True)
    capacity = 4 * token_count // owners
    flat_ids = expert_ids.reshape(-1)
    slot_list, slot_spot = place_rows(flat_ids, owners, capacity)
    features = lax.dynamic_slice_in_dim(
        tokens, lax.axis_index("tensor") * width_part, width_part, 1
    )
    outgoing = with_zero_row(features)[slot_list // 2]
    arrived = lax.all_to_all(outgoing, "dp", split_axis=0, concat_axis=0, tiled=True)
    gate_part = against(arrived, own[:, 0, :]).astype(jnp.bfloat16)
    up_part = against(arrived, own[:, 1, :]).astype(jnp.bfloat16)
    both = jnp.stack([gate_part, up_part], axis=1)
    summed = lax.psum_scatter(both, "tensor", scatter_dimension=0, tiled=True).astype(jnp.float32)
    hidden_part = (jax.nn.silu(summed[:, 0, :]) * summed[:, 1, :]).astype(jnp.bfloat16)
    hidden = lax.all_gather(hidden_part, "tensor", axis=0, tiled=True)
    expert_out = jnp.dot(hidden, own[:, 2, :], preferred_element_type=jnp.float32).astype(
        jnp.bfloat16
    )
    returned = lax.all_to_all(expert_out, "dp", split_axis=0, concat_axis=0, tiled=True)
    picked_out = returned[slot_spot].reshape(token_count, 2, width_part)
    mixed_out = jnp.sum(mixing[:, :, None] * picked_out.astype(jnp.float32), axis=1)
    return mixed_out.astype(jnp.bfloat16)


def solution(mesh):
    in_specs = (
        P("dp", None),
        P(),
        P(("dp", "tensor"), None),
        P(("dp", "tensor"), None),
        P(("dp", "tensor"), None),
        P("dp", None),
        P("dp", None),
    )
    out_specs = P("dp", "tensor")
    return jax.shard_map(
        on_device, mesh=mesh, in_specs=in_specs, out_specs=out_specs, check_vma=False
    )
```

profile of v0, /device:TPU:1, one launch (start us, length us, event | category | flops | bytes accessed | tf_op | source)
XLA Modules:
  0.0 451.2 jit_solution(5226104023529939072)
XLA Ops:
  6.5 2.1 pad_maximum_fusion.1
  8.6 8.4 %copy.72 = bf16[56,3,8192]{0,1,2:T(4,128)(2,1)} copy(bf16[56,3,8192]{2,0,1:T(8,128)(2,1)S(1)} %pad_maximum_fusion.1) | data formatting | bytes 5505024 | tf_op jit(solution)/shard_map/stack | solution.py:37
  17.0 12.4 %reshape.154 = bf16[8,2,86016]{2,1,0:T(2,128)(2,1)} reshape(bf16[8192,3,56]{2,1,0:T(4,128)(2,1)} %bitcast.87) | data formatting | bytes 5505024
  29.4 9.1 %all-to-all-start.1 = ((bf16[8,2,86016]{2,1,0:T(2,128)(2,1)}), bf16[8,2,86016]{2,1,0:T(2,128)(2,1)S(1)}, u32[]{:S(2)}, u32[]{:S(2)}) async-start(bf16[8,2,86016]{2,1,0:T(2,128)(2,1)} %reshape.154), calls=%async_computation.1 | async-start | bytes 5505024 | tf_op jit(solution)/shard_map/all_to_all | solution.py:38
  38.6 1.2 reduce-window.16
  40.2 2.9 scatter_custom_fusion.1
  43.1 61.2 %all-to-all-done.1 = bf16[8,2,86016]{2,1,0:T(2,128)(2,1)S(1)} async-done(((bf16[8,2,86016]{2,1,0:T(2,128)(2,1)}), bf16[8,2,86016]{2,1,0:T(2,128)(2,1)S(1)}, u32[]{:S(2)}, u32[]{:S(2)}) %all-to-all-start.1) | async-done | bytes 2752544 | tf_op jit(solution)/shard_map/all_to_all | solution.py:38
  104.3 13.2 %reshape.155 = bf16[8192,3,56]{2,1,0:T(4,128)(2,1)} reshape(bf16[8,2,86016]{2,1,0:T(2,128)(2,1)S(1)} %all-to-all-done.1) | data formatting | bytes 5505024
  117.5 10.6 %copy.79 = bf16[56,3,8,1024]{3,0,2,1:T(8,128)(2,1)S(1)} copy(bf16[56,3,8,1024]{0,1,3,2:T(4,128)(2,1)} %bitcast.88) | data formatting | bytes 5505024 | tf_op jit(solution)/shard_map/all_to_all | solution.py:38
  128.1 2.4 copy.75
  130.5 3.2 concatenate.7
  133.7 33.1 %gather_fusion.1 = bf16[896,3,1024]{2,1,0:T(4,128)(2,1)} fusion(bf16[449,3,1024]{2,1,0:T(4,128)(2,1)} %concatenate.7, s32[1024]{0:T(1024)S(1)} %pad_clamp_fusion.1), kind=kCustom, calls=%fused_computation.1 | custom fusion | bytes 11013632 | tf_op jit(solution)/shard_map/gather | solution.py:41
  166.8 7.6 %all-to-all-start.2 = ((bf16[896,3,1024]{2,1,0:T(4,128)(2,1)}), bf16[896,3,1024]{2,1,0:T(4,128)(2,1)}, u32[]{:S(2)}, u32[]{:S(2)}) async-start(bf16[896,3,1024]{2,1,0:T(4,128)(2,1)} %gather_fusion.1), calls=%async_computation.2 | async-start | bytes 14680064 | tf_op jit(solution)/shard_map/all_to_all | solution.py:42
  177.9 2.4 scatter_custom_fusion
  180.4 5.4 %gather_fusion = bf16[1024,1024]{1,0:T(8,128)(2,1)} fusion(bf16[257,1024]{1,0:T(8,128)(2,1)S(1)} %concatenate.6, s32[1024]{0:T(1024)S(1)} %fusion.21), kind=kCustom, calls=%fused_computation | custom fusion | bytes 4198400 | tf_op jit(solution)/shard_map/gather | solution.py:49
  185.7 75.9 %all-to-all-done.2 = bf16[896,3,1024]{2,1,0:T(4,128)(2,1)} async-done(((bf16[896,3,1024]{2,1,0:T(4,128)(2,1)}), bf16[896,3,1024]{2,1,0:T(4,128)(2,1)}, u32[]{:S(2)}, u32[]{:S(2)}) %all-to-all-start.2) | async-done | bytes 5505056 | tf_op jit(solution)/shard_map/all_to_all | solution.py:42
  261.6 8.7 %all-to-all-start = ((bf16[32,32,1024]{2,1,0:T(8,128)(2,1)}), bf16[32,32,1024]{2,1,0:T(8,128)(2,1)S(1)}, u32[]{:S(2)}, u32[]{:S(2)}) async-start(bf16[32,32,1024]{2,1,0:T(8,128)(2,1)} %bitcast.4), calls=%async_computation | async-start | bytes 4194304 | tf_op jit(solution)/shard_map/all_to_all | solution.py:50
  270.4 18.2 %fusion.28 = (bf16[896,1,1024]{2,1,0:T(2,128)(2,1)}, bf16[896,1,1024]{2,1,0:T(2,128)(2,1)}, bf16[896,1,1024]{2,1,0:T(2,128)(2,1)}) fusion(bf16[896,3,1024]{2,1,0:T(4,128)(2,1)} %all-to-all-done.2), kind=kLoop, calls=%fused_computation.70 | loop fusion | bytes 11010048 | tf_op jit(solution)/shard_map/slice | solution.py:57
  288.6 10.0 %all-to-all-done = bf16[32,32,1024]{2,1,0:T(8,128)(2,1)S(1)} async-done(((bf16[32,32,1024]{2,1,0:T(8,128)(2,1)}), bf16[32,32,1024]{2,1,0:T(8,128)(2,1)S(1)}, u32[]{:S(2)}, u32[]{:S(2)}) %all-to-all-start) | async-done | bytes 2097184 | tf_op jit(solution)/shard_map/all_to_all | solution.py:50
  298.6 4.6 %convert_bitcast_fusion.1 = bf16[1024,1,896]{2,0,1:T(8,128)(2,1)S(1)} fusion(bf16[1024,1024]{1,0:T(8,128)(2,1)S(1)} %bitcast.91, bf16[896,1,1024]{2,1,0:T(2,128)(2,1)} %get-tuple-element.9), kind=kOutput, calls=%fused_computation.19 | convolution fusion | flops 1879965696 | bytes 5767168 | tf_op jit(solution)/shard_map/dot_general | solution.py:24
  303.2 2.4 convert_bitcast_fusion
  305.6 2.2 pad_maximum_fusion
  307.9 44.0 %reduce-scatter.2.cloned.1.call-done = bf16[128,2,896]{2,0,1:T(8,128)(2,1)} async-done(((bf16[1024,2,896]{2,0,1:T(8,128)(2,1)}), bf16[128,2,896]{2,0,1:T(8,128)(2,1)}) %reduce-scatter.2.cloned.1.call-update) | async-done | bytes 458768 | tf_op jit(solution)/shard_map/reduce_scatter | solution.py:54
  353.8 35.5 %all-gather.2.cloned.1.call-done = bf16[1024,896]{1,0:T(8,128)(2,1)} async-done(((bf16[128,896]{1,0:T(8,128)(2,1)}), bf16[1024,896]{1,0:T(8,128)(2,1)}) %all-gather.2.cloned.1.call-update) | async-done | bytes 1835024 | tf_op jit(solution)/shard_map/all_gather | solution.py:56
  389.3 6.3 %convolution_convert_fusion = bf16[1024,1024]{1,0:T(8,128)(2,1)} fusion(bf16[1024,896]{1,0:T(8,128)(2,1)} %all-gather.2.cloned.1.call-done, bf16[896,1,1024]{2,1,0:T(2,128)(2,1)} %get-tuple-element.7), kind=kOutput, calls=%fused_computation.9 | convolution fusion | flops 1880096768 | bytes 5767168 | tf_op jit(solution)/shard_map/dot_general | solution.py:57
  395.6 11.6 %all-to-all-start.3 = ((bf16[32,32,1024]{2,1,0:T(8,128)(2,1)}), bf16[32,32,1024]{2,1,0:T(8,128)(2,1)S(1)}, u32[]{:S(2)}, u32[]{:S(2)}) async-start(bf16[32,32,1024]{2,1,0:T(8,128)(2,1)} %bitcast.90), calls=%async_computation.4 | async-start | bytes 4194304 | tf_op jit(solution)/shard_map/all_to_all | solution.py:60
  407.5 3.5 fusion.29
  411.1 4.5 %gather_fusion.3 = f32[512]{0:T(512)S(1)} fusion(f32[256,32]{0,1:T(8,128)S(1)} %fusion.29, s32[512]{0:T(512)S(1)} %reshape.119), kind=kCustom, calls=%fused_computation.3 | custom fusion | bytes 8192 | tf_op jit(solution)/shard_map/jit(take_along_axis)/gather | solution.py:35
  416.1 19.6 %all-to-all-done.3 = bf16[32,32,1024]{2,1,0:T(8,128)(2,1)S(1)} async-done(((bf16[32,32,1024]{2,1,0:T(8,128)(2,1)}), bf16[32,32,1024]{2,1,0:T(8,128)(2,1)S(1)}, u32[]{:S(2)}, u32[]{:S(2)}) %all-to-all-start.3) | async-done | bytes 2097184 | tf_op jit(solution)/shard_map/all_to_all | solution.py:60
  435.7 2.8 gather_fusion.2
  438.5 2.4 reshape.94
  440.9 3.5 multiply_reduce_fusion
  (53 shorter events, 6.5 us)
Async XLA Ops:
  6.5 401.0 %copy-start = (bf16[8192,32]{0,1:T(8,128)(2,1)S(1)}, bf16[8192,32]{0,1:T(8,128)(2,1)}, u32[]{:S(2)}) copy-start(bf16[8192,32]{0,1:T(8,128)(2,1)} %param.8) | copy-start | bytes 1572868
  29.4 9.1 %copy-start.4 = (s32[448,1]{0,1:T(1,128)S(1)}, s32[448,1]{0,1:T(1,128)}, u32[]{:S(2)}) copy-start(s32[448,1]{0,1:T(1,128)} %param.12) | copy-start | bytes 5380
  29.4 74.9 %all-to-all-start.1 = ((bf16[8,2,86016]{2,1,0:T(2,128)(2,1)}), bf16[8,2,86016]{2,1,0:T(2,128)(2,1)S(1)}, u32[]{:S(2)}, u32[]{:S(2)}) async-start(bf16[8,2,86016]{2,1,0:T(2,128)(2,1)} %reshape.154), calls=%async_computation.1 | async-start | bytes 5505024 | tf_op jit(solution)/shard_map/all_to_all | solution.py:38
  166.8 7.7 %copy-start.3 = (s32[256,2]{0,1:T(2,128)S(1)}, s32[256,2]{0,1:T(2,128)}, u32[]{:S(2)}) copy-start(s32[256,2]{0,1:T(2,128)} %param.13) | copy-start | bytes 6148
  166.8 94.8 %all-to-all-start.2 = ((bf16[896,3,1024]{2,1,0:T(4,128)(2,1)}), bf16[896,3,1024]{2,1,0:T(4,128)(2,1)}, u32[]{:S(2)}, u32[]{:S(2)}) async-start(bf16[896,3,1024]{2,1,0:T(4,128)(2,1)} %gather_fusion.1), calls=%async_computation.2 | async-start | bytes 14680064 | tf_op jit(solution)/shard_map/all_to_all | solution.py:42
  261.6 37.0 %all-to-all-start = ((bf16[32,32,1024]{2,1,0:T(8,128)(2,1)}), bf16[32,32,1024]{2,1,0:T(8,128)(2,1)S(1)}, u32[]{:S(2)}, u32[]{:S(2)}) async-start(bf16[32,32,1024]{2,1,0:T(8,128)(2,1)} %bitcast.4), calls=%async_computation | async-start | bytes 4194304 | tf_op jit(solution)/shard_map/all_to_all | solution.py:50
  270.3 81.6 %reduce-scatter.2.cloned.1.call-start = ((), (), s32[]{:S(2)}) async-start(), calls=%async_computation.5 | async-start | bytes 4128768 | tf_op jit(solution)/shard_map/reduce_scatter | solution.py:54
  298.6 4.6 %copy-start.2 = (bf16[896,1,1024]{2,1,0:T(2,128)(2,1)S(1)}, bf16[896,1,1024]{2,1,0:T(2,128)(2,1)}, u32[]{:S(2)}) copy-start(bf16[896,1,1024]{2,1,0:T(2,128)(2,1)} %get-tuple-element.8) | copy-start | bytes 5505028
  307.8 81.5 %all-gather.2.cloned.1.call-start = ((), (), s32[]{:S(2)}) async-start(), calls=%async_computation.6 | async-start | bytes 2064384 | tf_op jit(solution)/shard_map/all_gather | solution.py:56
  395.6 40.1 %all-to-all-start.3 = ((bf16[32,32,1024]{2,1,0:T(8,128)(2,1)}), bf16[32,32,1024]{2,1,0:T(8,128)(2,1)S(1)}, u32[]{:S(2)}, u32[]{:S(2)}) async-start(bf16[32,32,1024]{2,1,0:T(8,128)(2,1)} %bitcast.90), calls=%async_computation.4 | async-start | bytes 4194304 | tf_op jit(solution)/shard_map/all_to_all | solution.py:60
  435.7 8.6 %copy-start.1 = (bf16[8192,32]{0,1:T(8,128)(2,1)S(1)}, bf16[8192,32]{0,1:T(8,128)(2,1)}, u32[]{:S(2)}) copy-start(bf16[8192,32]{0,1:T(8,128)(2,1)} %param.8) | copy-start | bytes 1572868
Sparse Core Ops, SparseCore 0:
  307.9 43.9 reduce-scatter.1
  353.9 35.3 all-gather.1
where the time goes:
time: 452 us; the launch traced here: 451 us
  waiting for transfers between devices  246 us (54%)
  local copies, waits for them, and re-layouts  125 us (28%)
  starting transfers between devices  37.2 us (8%)
  matrix products  16.8 us (4%)
  between operations  13.8 us (3%)
  other arithmetic  12.4 us (3%)
    all_to_all x1, waiting for transfers between devices, on_device(): own = lax.all_to_all(pick, 'dp', split_axis=0, concat_axis=0, tiled=True)  75.9 us
    all_to_all x1, waiting for transfers between devices, on_device(): lax.all_to_all(stacked, 'tensor', split_axis=2, concat_axis=0, tiled=True)  61.2 us
    reduce_scatter x1, waiting for transfers between devices, on_device(): lax.psum_scatter(both, 'tensor', scatter_dimension=0, tiled=True)  44 us
    all_gather x1, waiting for transfers between devices, on_device(): hidden = lax.all_gather(hidden_part, 'tensor', axis=0, tiled=True)  35.5 us
    gather x1, local copies, waits for them, and re-layouts, on_device(): pick = with_zero_row(rows)[unit_list]  33.1 us
    unnamed x13, local copies, waits for them, and re-layouts  25.7 us
    all_to_all x1, waiting for transfers between devices, on_device(): lax.all_to_all(expert_out, 'dp', split_axis=0, concat_axis=0, tiled=True)  19.6 us
    slice x1, local copies, waits for them, and re-layouts, on_device(): own[:, 2, :]  18.2 us
  transfers between devices with their start and end apart: 6, of which 6 were waited for; matrix products, arithmetic and copies ran while one was open for 9% of the time, Pallas kernels for 0%

commit v1 on v0

--- a/solution.py
+++ b/solution.py
@@ -53,7 +53,9 @@
     both = jnp.stack([gate_part, up_part], axis=1)
     summed = lax.psum_scatter(both, "tensor", scatter_dimension=0, tiled=True).astype(jnp.float32)
     hidden_part = (jax.nn.silu(summed[:, 0, :]) * summed[:, 1, :]).astype(jnp.bfloat16)
-    hidden = lax.all_gather(hidden_part, "tensor", axis=0, tiled=True)
+    hidden = jnp.concatenate(
+        lax.all_to_all(jnp.stack([hidden_part] * lax.axis_size("tensor")), "tensor", 0, 0), axis=0
+    )
     expert_out = jnp.dot(hidden, own[:, 2, :], preferred_element_type=jnp.float32).astype(
         jnp.bfloat16
     )

time: 452 us -> 468 us (1.035); the launches traced: 451 us -> 460 us
  blocking collectives: 0 us -> 48.1 us
  waiting for transfers between devices: 246 us -> 211 us
    all_to_all x0 -> x1, blocking collectives: none -> 48.1 us  [on_device(): lax.all_to_all(jnp.stack([hidden_part] * lax.axis_size('tensor')), 'tenso...]
    all_gather x1 -> x0, waiting for transfers between devices: 35.5 us -> none  [on_device(): hidden = lax.all_gather(hidden_part, 'tensor', axis=0, tiled=True)]
  transfers between devices with their start and end apart: 6 -> 5, of which waited for: 6 -> 5; matrix products, arithmetic and copies ran while one was open for 9% -> 9% of each run, Pallas kernels for 0% -> 0%
where the time goes in v1:
time: 468 us; the launch traced here: 460 us
  waiting for transfers between devices  211 us (45%)
  local copies, waits for them, and re-layouts  125 us (27%)
  blocking collectives  48.1 us (10%)
  starting transfers between devices  35.4 us (8%)
  matrix products  14.2 us (3%)
  between operations  14 us (3%)
  other arithmetic  11.7 us (2%)
    all_to_all x1, waiting for transfers between devices, on_device(): own = lax.all_to_all(pick, 'dp', split_axis=0, concat_axis=0, tiled=True)  75.9 us
    all_to_all x1, waiting for transfers between devices, on_device(): lax.all_to_all(stacked, 'tensor', split_axis=2, concat_axis=0, tiled=True)  61.2 us
    all_to_all x1, blocking collectives, on_device(): lax.all_to_all(jnp.stack([hidden_part] * lax.axis_size('tensor')), 'tenso...  48.1 us
    reduce_scatter x1, waiting for transfers between devices, on_device(): lax.psum_scatter(both, 'tensor', scatter_dimension=0, tiled=True)  44.1 us
    gather x1, local copies, waits for them, and re-layouts, on_device(): pick = with_zero_row(rows)[unit_list]  33.3 us
    unnamed x13, local copies, waits for them, and re-layouts  25.7 us
    all_to_all x1, waiting for transfers between devices, on_device(): lax.all_to_all(expert_out, 'dp', split_axis=0, concat_axis=0, tiled=True)  19.7 us
    slice x1, local copies, waits for them, and re-layouts, on_device(): own[:, 2, :]  18.2 us
  transfers between devices with their start and end apart: 5, of which 5 were waited for; matrix products, arithmetic and copies ran while one was open for 9% of the time, Pallas kernels for 0%

profile of v1, /device:TPU:1, one launch (start us, length us, event | category | flops | bytes accessed | tf_op | source)
XLA Modules:
  0.0 459.6 jit_solution(9944551154538953342)
XLA Ops:
  6.5 2.1 pad_maximum_fusion.1
  8.6 8.4 %copy.72 = bf16[56,3,8192]{0,1,2:T(4,128)(2,1)} copy(bf16[56,3,8192]{2,0,1:T(8,128)(2,1)S(1)} %pad_maximum_fusion.1) | data formatting | bytes 5505024 | tf_op jit(solution)/shard_map/stack | solution.py:37
  17.0 12.4 %reshape.163 = bf16[8,2,86016]{2,1,0:T(2,128)(2,1)} reshape(bf16[8192,3,56]{2,1,0:T(4,128)(2,1)} %bitcast.88) | data formatting | bytes 5505024
  29.4 9.1 %all-to-all-start.1 = ((bf16[8,2,86016]{2,1,0:T(2,128)(2,1)}), bf16[8,2,86016]{2,1,0:T(2,128)(2,1)S(1)}, u32[]{:S(2)}, u32[]{:S(2)}) async-start(bf16[8,2,86016]{2,1,0:T(2,128)(2,1)} %reshape.163), calls=%async_computation.1 | async-start | bytes 5505024 | tf_op jit(solution)/shard_map/all_to_all | solution.py:38
  38.6 1.2 reduce-window.16
  40.2 2.9 scatter_custom_fusion.1
  43.1 61.2 %all-to-all-done.1 = bf16[8,2,86016]{2,1,0:T(2,128)(2,1)S(1)} async-done(((bf16[8,2,86016]{2,1,0:T(2,128)(2,1)}), bf16[8,2,86016]{2,1,0:T(2,128)(2,1)S(1)}, u32[]{:S(2)}, u32[]{:S(2)}) %all-to-all-start.1) | async-done | bytes 2752544 | tf_op jit(solution)/shard_map/all_to_all | solution.py:38
  104.3 13.2 %reshape.164 = bf16[8192,3,56]{2,1,0:T(4,128)(2,1)} reshape(bf16[8,2,86016]{2,1,0:T(2,128)(2,1)S(1)} %all-to-all-done.1) | data formatting | bytes 5505024
  117.5 10.6 %copy.79 = bf16[56,3,8,1024]{3,0,2,1:T(8,128)(2,1)S(1)} copy(bf16[56,3,8,1024]{0,1,3,2:T(4,128)(2,1)} %bitcast.89) | data formatting | bytes 5505024 | tf_op jit(solution)/shard_map/all_to_all | solution.py:38
  128.1 2.4 copy.75
  130.5 3.2 concatenate.7
  133.7 33.3 %gather_fusion.1 = bf16[896,3,1024]{2,1,0:T(4,128)(2,1)} fusion(bf16[449,3,1024]{2,1,0:T(4,128)(2,1)} %concatenate.7, s32[1024]{0:T(1024)S(1)} %pad_clamp_fusion.1), kind=kCustom, calls=%fused_computation.1 | custom fusion | bytes 11013632 | tf_op jit(solution)/shard_map/gather | solution.py:41
  167.1 7.6 %all-to-all-start.2 = ((bf16[896,3,1024]{2,1,0:T(4,128)(2,1)}), bf16[896,3,1024]{2,1,0:T(4,128)(2,1)}, u32[]{:S(2)}, u32[]{:S(2)}) async-start(bf16[896,3,1024]{2,1,0:T(4,128)(2,1)} %gather_fusion.1), calls=%async_computation.2 | async-start | bytes 14680064 | tf_op jit(solution)/shard_map/all_to_all | solution.py:42
  178.2 2.4 scatter_custom_fusion
  180.6 5.4 %gather_fusion = bf16[1024,1024]{1,0:T(8,128)(2,1)} fusion(bf16[257,1024]{1,0:T(8,128)(2,1)S(1)} %concatenate.6, s32[1024]{0:T(1024)S(1)} %fusion.21), kind=kCustom, calls=%fused_computation | custom fusion | bytes 4198400 | tf_op jit(solution)/shard_map/gather | solution.py:49
  186.0 75.9 %all-to-all-done.2 = bf16[896,3,1024]{2,1,0:T(4,128)(2,1)} async-done(((bf16[896,3,1024]{2,1,0:T(4,128)(2,1)}), bf16[896,3,1024]{2,1,0:T(4,128)(2,1)}, u32[]{:S(2)}, u32[]{:S(2)}) %all-to-all-start.2) | async-done | bytes 5505056 | tf_op jit(solution)/shard_map/all_to_all | solution.py:42
  261.9 8.7 %all-to-all-start = ((bf16[32,32,1024]{2,1,0:T(8,128)(2,1)}), bf16[32,32,1024]{2,1,0:T(8,128)(2,1)S(1)}, u32[]{:S(2)}, u32[]{:S(2)}) async-start(bf16[32,32,1024]{2,1,0:T(8,128)(2,1)} %bitcast.4), calls=%async_computation | async-start | bytes 4194304 | tf_op jit(solution)/shard_map/all_to_all | solution.py:50
  270.7 18.2 %fusion.28 = (bf16[896,1,1024]{2,1,0:T(2,128)(2,1)}, bf16[896,1,1024]{2,1,0:T(2,128)(2,1)}, bf16[896,1,1024]{2,1,0:T(2,128)(2,1)}) fusion(bf16[896,3,1024]{2,1,0:T(4,128)(2,1)} %all-to-all-done.2), kind=kLoop, calls=%fused_computation.70 | loop fusion | bytes 11010048 | tf_op jit(solution)/shard_map/slice | solution.py:59
  288.9 10.1 %all-to-all-done = bf16[32,32,1024]{2,1,0:T(8,128)(2,1)S(1)} async-done(((bf16[32,32,1024]{2,1,0:T(8,128)(2,1)}), bf16[32,32,1024]{2,1,0:T(8,128)(2,1)S(1)}, u32[]{:S(2)}, u32[]{:S(2)}) %all-to-all-start) | async-done | bytes 2097184 | tf_op jit(solution)/shard_map/all_to_all | solution.py:50
  298.9 4.6 convert_bitcast_fusion.1
  303.5 2.4 convert_bitcast_fusion
  305.9 2.2 pad_maximum_fusion
  308.1 44.1 %reduce-scatter.2.cloned.1.call-done = bf16[128,2,896]{2,0,1:T(8,128)(2,1)} async-done(((bf16[1024,2,896]{2,0,1:T(8,128)(2,1)}), bf16[128,2,896]{2,0,1:T(8,128)(2,1)}) %reduce-scatter.2.cloned.1.call-update) | async-done | bytes 458768 | tf_op jit(solution)/shard_map/reduce_scatter | solution.py:54
  353.6 48.1 %all_to_all.52 = bf16[8,128,896]{2,1,0:T(8,128)(2,1)S(1)} all-to-all(bf16[8,128,896]{2,1,0:T(8,128)(2,1)S(1)} %stack.39), channel_id=1, replica_groups=mesh['dp'=32,'tensor'=8] {'tensor'}, dimensions={0} | all-to-all | bytes 3670016 | tf_op jit(solution)/shard_map/all_to_all | solution.py:57
  401.8 3.7 convolution_convert_fusion
  405.5 9.8 %all-to-all-start.4 = ((bf16[32,32,1024]{2,1,0:T(8,128)(2,1)}), bf16[32,32,1024]{2,1,0:T(8,128)(2,1)S(1)}, u32[]{:S(2)}, u32[]{:S(2)}) async-start(bf16[32,32,1024]{2,1,0:T(8,128)(2,1)} %bitcast.91), calls=%async_computation.5 | async-start | bytes 4194304 | tf_op jit(solution)/shard_map/all_to_all | solution.py:62
  415.6 3.5 fusion.29
  419.2 4.5 gather_fusion.3
  424.2 19.7 %all-to-all-done.4 = bf16[32,32,1024]{2,1,0:T(8,128)(2,1)S(1)} async-done(((bf16[32,32,1024]{2,1,0:T(8,128)(2,1)}), bf16[32,32,1024]{2,1,0:T(8,128)(2,1)S(1)}, u32[]{:S(2)}, u32[]{:S(2)}) %all-to-all-start.4) | async-done | bytes 2097184 | tf_op jit(solution)/shard_map/all_to_all | solution.py:62
  443.8 2.8 gather_fusion.2
  446.6 2.4 reshape.103
  449.0 3.5 multiply_reduce_fusion
  (52 shorter events, 6.0 us)
Async XLA Ops:
  6.5 409.1 %copy-start = (bf16[8192,32]{0,1:T(8,128)(2,1)S(1)}, bf16[8192,32]{0,1:T(8,128)(2,1)}, u32[]{:S(2)}) copy-start(bf16[8192,32]{0,1:T(8,128)(2,1)} %param.8) | copy-start | bytes 1572868
  29.4 9.1 %copy-start.4 = (s32[448,1]{0,1:T(1,128)S(1)}, s32[448,1]{0,1:T(1,128)}, u32[]{:S(2)}) copy-start(s32[448,1]{0,1:T(1,128)} %param.12) | copy-start | bytes 5380
  29.4 74.9 %all-to-all-start.1 = ((bf16[8,2,86016]{2,1,0:T(2,128)(2,1)}), bf16[8,2,86016]{2,1,0:T(2,128)(2,1)S(1)}, u32[]{:S(2)}, u32[]{:S(2)}) async-start(bf16[8,2,86016]{2,1,0:T(2,128)(2,1)} %reshape.163), calls=%async_computation.1 | async-start | bytes 5505024 | tf_op jit(solution)/shard_map/all_to_all | solution.py:38
  167.1 7.7 %copy-start.3 = (s32[256,2]{0,1:T(2,128)S(1)}, s32[256,2]{0,1:T(2,128)}, u32[]{:S(2)}) copy-start(s32[256,2]{0,1:T(2,128)} %param.13) | copy-start | bytes 6148
  167.1 94.8 %all-to-all-start.2 = ((bf16[896,3,1024]{2,1,0:T(4,128)(2,1)}), bf16[896,3,1024]{2,1,0:T(4,128)(2,1)}, u32[]{:S(2)}, u32[]{:S(2)}) async-start(bf16[896,3,1024]{2,1,0:T(4,128)(2,1)} %gather_fusion.1), calls=%async_computation.2 | async-start | bytes 14680064 | tf_op jit(solution)/shard_map/all_to_all | solution.py:42
  261.9 37.0 %all-to-all-start = ((bf16[32,32,1024]{2,1,0:T(8,128)(2,1)}), bf16[32,32,1024]{2,1,0:T(8,128)(2,1)S(1)}, u32[]{:S(2)}, u32[]{:S(2)}) async-start(bf16[32,32,1024]{2,1,0:T(8,128)(2,1)} %bitcast.4), calls=%async_computation | async-start | bytes 4194304 | tf_op jit(solution)/shard_map/all_to_all | solution.py:50
  270.6 81.5 %reduce-scatter.2.cloned.1.call-start = ((), (), s32[]{:S(2)}) async-start(), calls=%async_computation.6 | async-start | bytes 4128768 | tf_op jit(solution)/shard_map/reduce_scatter | solution.py:54
  298.9 4.6 copy-start.2
  353.4 48.4 %copy-start.1 = (bf16[896,1,1024]{2,1,0:T(2,128)(2,1)S(1)}, bf16[896,1,1024]{2,1,0:T(2,128)(2,1)}, u32[]{:S(2)}) copy-start(bf16[896,1,1024]{2,1,0:T(2,128)(2,1)} %get-tuple-element.7) | copy-start | bytes 5505028
  405.5 38.3 %all-to-all-start.4 = ((bf16[32,32,1024]{2,1,0:T(8,128)(2,1)}), bf16[32,32,1024]{2,1,0:T(8,128)(2,1)S(1)}, u32[]{:S(2)}, u32[]{:S(2)}) async-start(bf16[32,32,1024]{2,1,0:T(8,128)(2,1)} %bitcast.91), calls=%async_computation.5 | async-start | bytes 4194304 | tf_op jit(solution)/shard_map/all_to_all | solution.py:62
Sparse Core Ops, SparseCore 0:
  308.2 43.9 reduce-scatter.1
